TPU v7x, 128 devices: a whole 4x4x4 slice. The times are simulated.
128 devices in a mesh: xb: 16 (over y, z), yb: 8 (over x, core).
Axes of the slice: x: 4, y: 4, z: 4, core: 2. Of those that a mesh axis runs over, the one named last changes fastest.
Arguments:
- initial_guess: float32 [128, 512, 256], P('xb', 'yb'), may hold values from -4 to 4
- right_side: float32 [128, 512, 256], P('xb', 'yb'), may hold values from -8 to 8
- coefficient: float32 [128, 512, 256], P('xb', 'yb'), may hold values from 0.3 to 3
Outputs:
- fine_field: float32 [128, 512, 256], P('xb', 'yb')
- middle_field: float32 [64, 256, 128], P('xb', 'yb')
- lower_field: float32 [32, 128, 64], P('xb', 'yb')
- coarse_field: float32 [16, 64, 32], P('xb', 'yb')
All inputs are finite; a program needn't handle non-finite values.
Results may differ from a plain program's by a relative error of at most 0.00002.
Values sent between devices are 32-bit elements; how exact they have to be, the bound alone decides.
No kernel may reach another device: no remote copies, remote signals or barrier semaphores. Data moves between devices by JAX's collectives and lax.ppermute only.
A program may use at most 192 MiB of HBM per device.

v0:
```python
import jax
import jax.numpy as jnp
from jax import lax
from jax.sharding import PartitionSpec as P

COARSE_ITERS = 8
damping_alpha = 0.05
cheb_theta = 1.15
cheb_delta = 0.85
cheb_sigma = cheb_theta / cheb_delta
cheb_first = 1.0 / cheb_sigma
cheb_second = 1.0 / (2.0 * cheb_sigma - cheb_first)
cheb_carry = cheb_second * cheb_first
cheb_resid = 2.0 * cheb_second / cheb_delta
jacobi_weight = 0.8


def exchange(items, axis, dim, forwards=()):
    count = lax.axis_size(axis)
    low = [[] for _ in items]
    high = [[] for _ in items]
    boxes = [box for box, _, _ in forwards]
    reach = max((-(-width // block.shape[dim]) for block, width in items))
    for hop in range(1, reach + 1):
        for sign in (1, -1):
            pieces = []
            owners = []
            for index, (block, width) in enumerate(items):
                size = block.shape[dim]
                rows = min(size, width - (hop - 1) * size)
                if rows <= 0:
                    continue
                begin = size - rows if sign == 1 else 0
                pieces.append(lax.slice_in_dim(block, begin, begin + rows, axis=dim))
                owners.append(index)
            if hop == 1:
                for index, (box, rows_low, rows_high) in enumerate(forwards):
                    rows = rows_low if sign == 1 else rows_high
                    pieces.append(lax.slice_in_dim(box, rows[0], rows[1], axis=dim))
                    owners.append(-1 - index)
            common = [max((p.shape[d] for p in pieces)) for d in (1, 2)]
            joined = jnp.concatenate(
                [
                    jnp.pad(p, ((0, 0), (0, common[0] - p.shape[1]), (0, common[1] - p.shape[2])))
                    for p in pieces
                ],
                axis=0,
            )
            if sign == 1:
                pairs = [(i, i + hop) for i in range(count - hop)]
            else:
                pairs = [(i + hop, i) for i in range(count - hop)]
            got = lax.ppermute(joined, axis, pairs)
            offset = 0
            for index, piece in zip(owners, pieces):
                part = got[offset : offset + piece.shape[0], : piece.shape[1], : piece.shape[2]]
                offset += piece.shape[0]
                if index < 0:
                    box = boxes[-1 - index]
                    parts = [part, box] if sign == 1 else [box, part]
                    boxes[-1 - index] = jnp.concatenate(parts, axis=dim)
                elif sign == 1:
                    low[index].insert(0, part)
                else:
                    high[index].append(part)
    extended = [
        jnp.concatenate(low[i] + [block] + high[i], axis=dim)
        for i, (block, width) in enumerate(items)
    ]
    return (extended, boxes)


def pad_z(box):
    return jnp.pad(box, ((0, 0), (0, 0), (1, 1)))


def trim(box):
    return box[1:-1, 1:-1, :]


def neighbours(padded):
    return [
        padded[2:, 1:-1, 1:-1],
        padded[:-2, 1:-1, 1:-1],
        padded[1:-1, 2:, 1:-1],
        padded[1:-1, :-2, 1:-1],
        padded[1:-1, 1:-1, 2:],
        padded[1:-1, 1:-1, :-2],
    ]


def face_weights(padded_coef, scale):
    centre = padded_coef[1:-1, 1:-1, 1:-1]
    weights = [0.5 * scale * (centre + other) for other in neighbours(padded_coef)]
    diagonal = damping_alpha + weights[0]
    for other in weights[1:]:
        diagonal = diagonal + other
    return (weights, diagonal)


def apply_operator(padded, field, weights, diagonal):
    result = diagonal * field
    for weight, other in zip(weights, neighbours(padded)):
        result = result - weight * other
    return result


def smooth_level(start, right_side, coefficient, scale, extend):
    weights, diagonal = face_weights(extend(coefficient), scale)
    if start is None:
        start = jnp.zeros_like(right_side)
        residual = right_side
    else:
        residual = right_side - apply_operator(extend(start), start, weights, diagonal)
    first_step = residual / (cheb_theta * diagonal)
    first = start + first_step
    residual = right_side - apply_operator(extend(first), first, weights, diagonal)
    second_step = cheb_carry * first_step + cheb_resid * residual / diagonal
    second = first + second_step
    residual = right_side - apply_operator(extend(second), second, weights, diagonal)
    return (second, residual)


def pair_matrix(count):
    rows = jnp.arange(count // 2)[:, None]
    cols = jnp.arange(count)[None, :] // 2
    return (rows == cols).astype(jnp.float32)


def restrict_field(field):
    sx, sy, sz = field.shape
    halves = field.reshape(sx // 2, 2, sy, sz)
    summed = halves[:, 0] + halves[:, 1]
    summed = jnp.einsum("xyZ,zZ->xyz", summed, pair_matrix(sz), precision=lax.Precision.HIGHEST)
    pairs_y = jnp.broadcast_to(pair_matrix(sy), (sx // 2, sy // 2, sy))
    summed = jnp.einsum("xyY,xYz->xyz", pairs_y, summed, precision=lax.Precision.HIGHEST)
    return summed * 0.125


def coarse_solve(right_side, coefficient, scale, extend):
    weights, diagonal = face_weights(extend(coefficient), scale)
    field = jnp.zeros_like(right_side)
    for repeat in range(COARSE_ITERS):
        field = (
            field
            + jacobi_weight
            * (right_side - apply_operator(extend(field), field, weights, diagonal))
            / diagonal
        )
    leftover = right_side - apply_operator(extend(field), field, weights, diagonal)
    ones_field = jnp.ones_like(right_side)
    image_ones = apply_operator(extend(ones_field), ones_field, weights, diagonal)
    return field + jnp.sum(leftover) / jnp.sum(image_ones)


def extend_all(field):
    return jnp.pad(field, 1)


def box_weights(padded_coef, scale):
    centre = padded_coef[1:-1, 1:-1, 1:-1]
    outside = centre == 0.0
    weights = [
        jnp.where(outside, 0.0, 0.5 * scale * (centre + other)) for other in neighbours(padded_coef)
    ]
    diagonal = damping_alpha + weights[0]
    for other in weights[1:]:
        diagonal = diagonal + other
    return (weights, diagonal)


def smooth_box(start, right_side, coefficient, scale):
    weights, diagonal = box_weights(pad_z(coefficient), scale)
    if start is None:
        start = jnp.zeros_like(right_side)
        residual = right_side
    else:
        residual = right_side - apply_operator(pad_z(start), trim(start), weights, diagonal)
        start = trim(start)
    first_step = residual / (cheb_theta * diagonal)
    first = start + first_step
    weights = [trim(w) for w in weights]
    diagonal = trim(diagonal)
    right_side = trim(right_side)
    residual = right_side - apply_operator(pad_z(first), trim(first), weights, diagonal)
    second_step = cheb_carry * trim(first_step) + cheb_resid * residual / diagonal
    second = trim(first) + second_step
    weights = [trim(w) for w in weights]
    diagonal = trim(diagonal)
    residual = trim(right_side) - apply_operator(pad_z(second), trim(second), weights, diagonal)
    return (trim(second), residual)


def collect_grid(right_side, coefficient):
    sx, sy, sz = right_side.shape
    count_x = lax.axis_size("xb")
    count_y = lax.axis_size("yb")
    flat = jnp.concatenate([right_side.reshape(1, -1), coefficient.reshape(1, -1)], axis=1)
    both = lax.all_gather(flat, ("xb", "yb"), axis=0, tiled=True)
    size = sx * sy * sz
    return tuple(
        (
            piece.reshape(count_x, count_y, sx, sy, sz)
            .transpose(0, 2, 1, 3, 4)
            .reshape(count_x * sx, count_y * sy, sz)
            for piece in (both[:, :size], both[:, size:])
        )
    )


def own_block(whole, shape):
    start_x = lax.axis_index("xb") * shape[0]
    start_y = lax.axis_index("yb") * shape[1]
    return lax.dynamic_slice(whole, (start_x, start_y, jnp.int32(0)), shape)


def per_device(initial_guess, right_side, coefficient):
    mid_coef = restrict_field(coefficient)
    low_coef = restrict_field(mid_coef)
    low_size = low_coef.shape[0]
    low_first = min(3, low_size)
    assert low_first == 3 or 2 * low_size >= 3
    guess_b, rhs_b, coef_b, mid_coef_b, low_coef_b = exchange(
        [(initial_guess, 7), (right_side, 7), (coefficient, 7), (mid_coef, 3), (low_coef, 3)],
        "yb",
        1,
    )[0]
    guess_b, rhs_b, coef_b = exchange([(guess_b, 3), (rhs_b, 2), (coef_b, 3)], "xb", 0)[0]
    fine, fine_res = smooth_box(guess_b, rhs_b[:, 1:-1], coef_b, 1.0)
    fine = fine[:, 4:-4]
    mid_rhs = restrict_field(fine_res)
    mid_rhs_b, mid_coef_b, low_coef_b = exchange(
        [(mid_rhs, 2), (mid_coef_b, 3), (low_coef_b, low_first)], "xb", 0
    )[0]
    middle, mid_res = smooth_box(None, mid_rhs_b, mid_coef_b, 0.25)
    low_rhs = restrict_field(mid_res)
    (low_rhs_b,) = exchange([(low_rhs, 3)], "yb", 1)[0]
    forwards = ()
    if low_first < 3:
        forwards = ((low_coef_b, (2 * low_size - 3, low_size), (2 * low_size, low_size + 3)),)
    (low_rhs_b,), boxes = exchange([(low_rhs_b, 2)], "xb", 0, forwards)
    if low_first < 3:
        (low_coef_b,) = boxes
    lower, low_res = smooth_box(None, low_rhs_b[:, 1:-1], low_coef_b, 0.0625)
    coarse_rhs, coarse_coef = collect_grid(restrict_field(low_res), restrict_field(low_coef))
    coarse_whole = coarse_solve(coarse_rhs, coarse_coef, 0.015625, extend_all)
    sx, sy, sz = right_side.shape
    coarse = own_block(coarse_whole, (sx // 8, sy // 8, sz // 8))
    return (fine, middle, lower, coarse)


def solution(mesh):
    placed = (P("xb", "yb", None), P("xb", "yb", None), P("xb", "yb", None))
    return jax.shard_map(
        per_device,
        mesh=mesh,
        in_specs=placed,
        out_specs=(
            P("xb", "yb", None),
            P("xb", "yb", None),
            P("xb", "yb", None),
            P("xb", "yb", None),
        ),
        check_vma=False,
    )
```

profile of v0, /device:TPU:1, one launch (start us, length us, event | category | flops | bytes accessed | tf_op | source)
XLA Modules:
  0.0 128.3 jit_solution(8711913986575202182)
XLA Ops:
  0.7 1.0 slice_dynamic-update-slice_fusion.2
  1.7 1.3 %fusion.218 = f32[4,64,128]{2,1,0:T(8,128)S(1)} fusion(f32[4,2,64,256]{3,2,1,0:T(8,128)} %bitcast.81, s32[256]{0:T(256)S(1)} %and_select_fusion.4), kind=kOutput, calls=%fused_computation.335 | convolution fusion | flops 100761600 | bytes 656384 | tf_op jit(solution)/shard_map/xyZ,zZ->xyz/dot_general | solution.py:134
  3.6 0.9 slice_dynamic-update-slice_fusion.1
  4.5 4.5 %collective-permute-start = (f32[30,7,256]{2,1,0:T(8,128)S(1)}, f32[30,7,256]{2,1,0:T(8,128)S(1)}, u32[]{:S(2)}, u32[]{:S(2)}) collective-permute-start(f32[30,7,256]{2,1,0:T(8,128)S(1)} %constant_dynamic-update-slice_fusion), channel_id=1, source_target_pairs={{0,1},{1,2},{2,3},{3,4},{4,5},{5,6},{6,7},{8,9},{9,10},{10,11},{11... | collective-permute-start | bytes 645128 | tf_op jit(solution)/shard_map/ppermute | solution.py:53
  9.1 1.9 %collective-permute-start.1 = (f32[30,7,256]{2,1,0:T(8,128)S(1)}, f32[30,7,256]{2,1,0:T(8,128)S(1)}, u32[]{:S(2)}, u32[]{:S(2)}) collective-permute-start(f32[30,7,256]{2,1,0:T(8,128)S(1)} %constant_dynamic-update-slice_fusion.2), channel_id=1, source_target_pairs={{1,0},{2,1},{3,2},{4,3},{5,4},{6,5},{7,6},{9,8},{10,9},{11,10},{12... | collective-permute-start | bytes 645128 | tf_op jit(solution)/shard_map/ppermute | solution.py:53
  11.0 1.2 collective-permute-done
  12.2 0.3 copy_dynamic-update-slice_fusion.1
  12.6 4.0 %collective-permute-done.1 = f32[30,7,256]{2,1,0:T(8,128)S(1)} collective-permute-done((f32[30,7,256]{2,1,0:T(8,128)S(1)}, f32[30,7,256]{2,1,0:T(8,128)S(1)}, u32[]{:S(2)}, u32[]{:S(2)}) %collective-permute-start.1) | collective-permute-done | bytes 215072 | tf_op jit(solution)/shard_map/ppermute | solution.py:53
  16.8 0.3 copy_dynamic-update-slice_fusion
  17.2 0.6 copy-done.2
  17.8 0.3 copy_dynamic-update-slice_fusion.2
  18.5 3.6 %collective-permute-start.2 = (f32[8,78,256]{2,0,1:T(8,128)S(1)}, f32[8,78,256]{2,0,1:T(8,128)S(1)}, u32[]{:S(2)}, u32[]{:S(2)}) collective-permute-start(f32[8,78,256]{2,0,1:T(8,128)S(1)} %pad_maximum_fusion.3), channel_id=1, source_target_pairs={{0,8},{8,16},{16,24},{24,32},{32,40},{40,48},{48,56},{56,64},{64,7... | collective-permute-start | bytes 1916936 | tf_op jit(solution)/shard_map/ppermute | solution.py:53
  22.3 1.3 %collective-permute-start.3 = (f32[8,78,256]{2,0,1:T(8,128)S(1)}, f32[8,78,256]{2,0,1:T(8,128)S(1)}, u32[]{:S(2)}, u32[]{:S(2)}) collective-permute-start(f32[8,78,256]{2,0,1:T(8,128)S(1)} %pad_maximum_fusion.4), channel_id=1, source_target_pairs={{8,0},{16,8},{24,16},{32,24},{40,32},{48,40},{56,48},{64,56},{72,6... | collective-permute-start | bytes 1916936 | tf_op jit(solution)/shard_map/ppermute | solution.py:53
  23.7 8.9 %collective-permute-done.2 = f32[8,78,256]{2,0,1:T(8,128)S(1)} collective-permute-done((f32[8,78,256]{2,0,1:T(8,128)S(1)}, f32[8,78,256]{2,0,1:T(8,128)S(1)}, u32[]{:S(2)}, u32[]{:S(2)}) %collective-permute-start.2) | collective-permute-done | bytes 639008 | tf_op jit(solution)/shard_map/ppermute | solution.py:53
  32.7 4.3 %collective-permute-done.3 = f32[8,78,256]{2,0,1:T(8,128)S(1)} collective-permute-done((f32[8,78,256]{2,0,1:T(8,128)S(1)}, f32[8,78,256]{2,0,1:T(8,128)S(1)}, u32[]{:S(2)}, u32[]{:S(2)}) %collective-permute-start.3) | collective-permute-done | bytes 639008 | tf_op jit(solution)/shard_map/ppermute | solution.py:53
  37.3 1.6 %add_add_fusion = (f32[12,76,256]{2,0,1:T(8,128)S(1)}, f32[12,76,256]{2,0,1:T(8,128)S(1)}, f32[12,76,256]{2,0,1:T(8,128)S(1)}, f32[12,76,256]{2,0,1:T(8,128)S(1)...) fusion(f32[14,78,256]{2,0,1:T(8,128)S(1)} %pad_maximum_fusion.2), kind=kLoop, calls=%fused_computation.55 | loop fusion | flops 5836800 | bytes 14041088 | tf_op jit(solution)/shard_map/add | solution.py:168
  39.0 0.3 pad_maximum_fusion.1
  39.5 2.1 %slice_add_fusion.4 = (f32[12,76,256]{2,0,1:T(8,128)S(1)}, f32[12,76,256]{2,0,1:T(8,128)S(1)}) fusion(f32[14,78,256]{2,0,1:T(8,128)S(1)} %pad_maximum_fusion, f32[12,76,256]{2,0,1:T(8,128)S(1)} %get-tuple-element.42, f32[12,76,256]{2,0,1:T(8,128)S(1)} %get-tuple-element.43, f32[12,76,256]{2,0,1:T(8,128)S(1)} %get-tuple-element.41, ...), kind=kLoop, calls=%fused_computation.74 | loop fusion | flops 5369856 | bytes 18087936 | tf_op jit(solution)/shard_map/add | solution.py:181
  41.6 2.4 %fusion.31 = f32[10,74,256]{2,0,1:T(8,128)S(1)} fusion(f32[12,76,256]{2,0,1:T(8,128)S(1)} %get-tuple-element.44, f32[12,76,256]{2,0,1:T(8,128)S(1)} %get-tuple-element.42, f32[12,76,256]{2,0,1:T(8,128)S(1)} %get-tuple-element.43, f32[12,76,256]{2,0,1:T(8,128)S(1)} %get-tuple-element.41, f32[12,76,256]{2,0,1:T(8,128)S(1)} %get-tuple-element.40, ...), kind=kLoop, calls=%fused_computation.63 | loop fusion | flops 3599360 | bytes 18976768 | tf_op jit(solution)/shard_map/add | solution.py:187
  44.0 0.9 fusion.40
  45.0 0.3 reshape.333
  45.3 0.5 fusion.365
  45.8 0.3 fusion.213
  46.1 0.3 convolution_multiply_fusion
  46.5 3.5 %collective-permute-start.4 = (f32[7,38,128]{2,1,0:T(8,128)S(1)}, f32[7,38,128]{2,1,0:T(8,128)S(1)}, u32[]{:S(2)}, u32[]{:S(2)}) collective-permute-start(f32[7,38,128]{2,1,0:T(8,128)S(1)} %get-tuple-element.89), channel_id=1, source_target_pairs={{0,8},{8,16},{16,24},{24,32},{32,40},{40,48},{48,56},{56,64},{64,7... | collective-permute-start | bytes 408584 | tf_op jit(solution)/shard_map/ppermute | solution.py:53
  50.0 1.3 %collective-permute-start.5 = (f32[7,38,128]{2,1,0:T(8,128)S(1)}, f32[7,38,128]{2,1,0:T(8,128)S(1)}, u32[]{:S(2)}, u32[]{:S(2)}) collective-permute-start(f32[7,38,128]{2,1,0:T(8,128)S(1)} %get-tuple-element.90), channel_id=1, source_target_pairs={{8,0},{16,8},{24,16},{32,24},{40,32},{48,40},{56,48},{64,56},{72,6... | collective-permute-start | bytes 408584 | tf_op jit(solution)/shard_map/ppermute | solution.py:53
  51.4 0.6 collective-permute-done.4
  52.0 3.8 %collective-permute-done.5 = f32[7,38,128]{2,1,0:T(8,128)S(1)} collective-permute-done((f32[7,38,128]{2,1,0:T(8,128)S(1)}, f32[7,38,128]{2,1,0:T(8,128)S(1)}, u32[]{:S(2)}, u32[]{:S(2)}) %collective-permute-start.5) | collective-permute-done | bytes 136224 | tf_op jit(solution)/shard_map/ppermute | solution.py:53
  56.3 0.7 fusion.272
  57.3 8.1 %collective-permute-start.6 = (f32[2,3,64]{2,1,0:T(4,128)S(1)}, f32[2,3,64]{2,1,0:T(4,128)S(1)}, u32[]{:S(2)}, u32[]{:S(2)}) collective-permute-start(f32[2,3,64]{2,1,0:T(4,128)S(1)} %get-tuple-element.91), channel_id=1, source_target_pairs={{0,1},{1,2},{2,3},{3,4},{4,5},{5,6},{6,7},{8,9},{9,10},{10,11},{11... | collective-permute-start | bytes 4616 | tf_op jit(solution)/shard_map/ppermute | solution.py:53
  65.4 1.9 %collective-permute-start.7 = (f32[2,3,64]{2,1,0:T(4,128)S(1)}, f32[2,3,64]{2,1,0:T(4,128)S(1)}, u32[]{:S(2)}, u32[]{:S(2)}) collective-permute-start(f32[2,3,64]{2,1,0:T(4,128)S(1)} %get-tuple-element.92), channel_id=1, source_target_pairs={{1,0},{2,1},{3,2},{4,3},{5,4},{6,5},{7,6},{9,8},{10,9},{11,10},{12... | collective-permute-start | bytes 4616 | tf_op jit(solution)/shard_map/ppermute | solution.py:53
  67.4 3.0 %collective-permute-done.7 = f32[2,3,64]{2,1,0:T(4,128)S(1)} collective-permute-done((f32[2,3,64]{2,1,0:T(4,128)S(1)}, f32[2,3,64]{2,1,0:T(4,128)S(1)}, u32[]{:S(2)}, u32[]{:S(2)}) %collective-permute-start.7) | collective-permute-done | bytes 1568 | tf_op jit(solution)/shard_map/ppermute | solution.py:53
  70.4 3.8 %collective-permute-start.8 = (f32[3,22,64]{2,1,0:T(8,128)S(1)}, f32[3,22,64]{2,1,0:T(8,128)S(1)}, u32[]{:S(2)}, u32[]{:S(2)}) collective-permute-start(f32[3,22,64]{2,1,0:T(8,128)S(1)} %get-tuple-element.87), channel_id=1, source_target_pairs={{0,8},{8,16},{16,24},{24,32},{32,40},{40,48},{48,56},{56,64},{64,7... | collective-permute-start | bytes 50696 | tf_op jit(solution)/shard_map/ppermute | solution.py:53
  74.5 1.0 copy.24
  75.4 1.5 %collective-permute-start.9 = (f32[3,22,64]{2,1,0:T(8,128)S(1)}, f32[3,22,64]{2,1,0:T(8,128)S(1)}, u32[]{:S(2)}, u32[]{:S(2)}) collective-permute-start(f32[3,22,64]{2,1,0:T(8,128)S(1)} %get-tuple-element.88), channel_id=1, source_target_pairs={{8,0},{16,8},{24,16},{32,24},{40,32},{48,40},{56,48},{64,56},{72,6... | collective-permute-start | bytes 50696 | tf_op jit(solution)/shard_map/ppermute | solution.py:53
  77.0 3.1 %collective-permute-done.9 = f32[3,22,64]{2,1,0:T(8,128)S(1)} collective-permute-done((f32[3,22,64]{2,1,0:T(8,128)S(1)}, f32[3,22,64]{2,1,0:T(8,128)S(1)}, u32[]{:S(2)}, u32[]{:S(2)}) %collective-permute-start.9) | collective-permute-done | bytes 16928 | tf_op jit(solution)/shard_map/ppermute | solution.py:53
  80.4 0.6 fusion.311
  81.4 37.1 %all-gather = f32[128,1,512]{2,1,0:T(1,128)S(1)} all-gather(f32[1,1,512]{2,1,0:T(1,128)S(1)} %maximum_bitcast_fusion), channel_id=1, replica_groups=mesh['xb'=16,'yb'=8] {'xb','yb'}, dimensions={0}, use_global_device_ids=true | all-gather | bytes 264192 | tf_op jit(solution)/shard_map/all_gather | solution.py:199
  118.9 1.0 fusion.192
  119.9 0.7 fusion.68
  120.6 0.7 fusion.84
  121.3 0.7 fusion.100
  122.0 0.7 fusion.116
  122.7 0.7 fusion.132
  123.3 0.7 fusion.148
  124.0 0.7 fusion.164
  124.8 1.6 %fusion.210 = (f32[]{:T(128)}, f32[]{:T(128)}) fusion(f32[16,64,32]{2,1,0:T(8,128)S(1)} %get-tuple-element.11, f32[16,64,32]{2,1,0:T(8,128)S(1)} %broadcast_in_dim.37, f32[16,64,32]{2,1,0:T(8,128)S(1)} %get-tuple-element.12, f32[16,64,32]{2,1,0:T(8,128)S(1)} %get-tuple-element.13, f32[16,64,32]{2,1,0:T(8,128)S(1)} %get-tuple-element.14, ...), kind=kLoop, calls=%fused_computation.320 | loop fusion | flops 1114110 | bytes 1179656 | tf_op jit(solution)/shard_map/reduce_sum | solution.py:153
  127.6 0.6 dynamic-slice_add_fusion
  (91 shorter events, 4.8 us)
Async XLA Ops:
  0.6 3.9 %copy-start = (f32[8,64,256]{2,1,0:T(8,128)S(1)}, f32[8,64,256]{2,1,0:T(8,128)}, u32[]{:S(2)}) copy-start(f32[8,64,256]{2,1,0:T(8,128)} %param.5) | copy-start | bytes 1572868
  0.6 11.6 %copy-start.1 = (f32[8,64,256]{2,1,0:T(8,128)S(1)}, f32[8,64,256]{2,1,0:T(8,128)}, u32[]{:S(2)}) copy-start(f32[8,64,256]{2,1,0:T(8,128)} %param.4) | copy-start | bytes 1572868
  4.5 7.6 %collective-permute-start = (f32[30,7,256]{2,1,0:T(8,128)S(1)}, f32[30,7,256]{2,1,0:T(8,128)S(1)}, u32[]{:S(2)}, u32[]{:S(2)}) collective-permute-start(f32[30,7,256]{2,1,0:T(8,128)S(1)} %constant_dynamic-update-slice_fusion), channel_id=1, source_target_pairs={{0,1},{1,2},{2,3},{3,4},{4,5},{5,6},{6,7},{8,9},{9,10},{10,11},{11... | collective-permute-start | bytes 645128 | tf_op jit(solution)/shard_map/ppermute | solution.py:53
  9.1 7.5 %collective-permute-start.1 = (f32[30,7,256]{2,1,0:T(8,128)S(1)}, f32[30,7,256]{2,1,0:T(8,128)S(1)}, u32[]{:S(2)}, u32[]{:S(2)}) collective-permute-start(f32[30,7,256]{2,1,0:T(8,128)S(1)} %constant_dynamic-update-slice_fusion.2), channel_id=1, source_target_pairs={{1,0},{2,1},{3,2},{4,3},{5,4},{6,5},{7,6},{9,8},{10,9},{11,10},{12... | collective-permute-start | bytes 645128 | tf_op jit(solution)/shard_map/ppermute | solution.py:53
  16.7 1.0 copy-start.2
  18.5 14.1 %collective-permute-start.2 = (f32[8,78,256]{2,0,1:T(8,128)S(1)}, f32[8,78,256]{2,0,1:T(8,128)S(1)}, u32[]{:S(2)}, u32[]{:S(2)}) collective-permute-start(f32[8,78,256]{2,0,1:T(8,128)S(1)} %pad_maximum_fusion.3), channel_id=1, source_target_pairs={{0,8},{8,16},{16,24},{24,32},{32,40},{40,48},{48,56},{56,64},{64,7... | collective-permute-start | bytes 1916936 | tf_op jit(solution)/shard_map/ppermute | solution.py:53
  22.3 14.6 %collective-permute-start.3 = (f32[8,78,256]{2,0,1:T(8,128)S(1)}, f32[8,78,256]{2,0,1:T(8,128)S(1)}, u32[]{:S(2)}, u32[]{:S(2)}) collective-permute-start(f32[8,78,256]{2,0,1:T(8,128)S(1)} %pad_maximum_fusion.4), channel_id=1, source_target_pairs={{8,0},{16,8},{24,16},{32,24},{40,32},{48,40},{56,48},{64,56},{72,6... | collective-permute-start | bytes 1916936 | tf_op jit(solution)/shard_map/ppermute | solution.py:53
  46.5 5.6 %collective-permute-start.4 = (f32[7,38,128]{2,1,0:T(8,128)S(1)}, f32[7,38,128]{2,1,0:T(8,128)S(1)}, u32[]{:S(2)}, u32[]{:S(2)}) collective-permute-start(f32[7,38,128]{2,1,0:T(8,128)S(1)} %get-tuple-element.89), channel_id=1, source_target_pairs={{0,8},{8,16},{16,24},{24,32},{32,40},{40,48},{48,56},{56,64},{64,7... | collective-permute-start | bytes 408584 | tf_op jit(solution)/shard_map/ppermute | solution.py:53
  50.0 5.8 %collective-permute-start.5 = (f32[7,38,128]{2,1,0:T(8,128)S(1)}, f32[7,38,128]{2,1,0:T(8,128)S(1)}, u32[]{:S(2)}, u32[]{:S(2)}) collective-permute-start(f32[7,38,128]{2,1,0:T(8,128)S(1)} %get-tuple-element.90), channel_id=1, source_target_pairs={{8,0},{16,8},{24,16},{32,24},{40,32},{48,40},{56,48},{64,56},{72,6... | collective-permute-start | bytes 408584 | tf_op jit(solution)/shard_map/ppermute | solution.py:53
  57.3 10.0 %collective-permute-start.6 = (f32[2,3,64]{2,1,0:T(4,128)S(1)}, f32[2,3,64]{2,1,0:T(4,128)S(1)}, u32[]{:S(2)}, u32[]{:S(2)}) collective-permute-start(f32[2,3,64]{2,1,0:T(4,128)S(1)} %get-tuple-element.91), channel_id=1, source_target_pairs={{0,1},{1,2},{2,3},{3,4},{4,5},{5,6},{6,7},{8,9},{9,10},{10,11},{11... | collective-permute-start | bytes 4616 | tf_op jit(solution)/shard_map/ppermute | solution.py:53
  65.4 4.9 %collective-permute-start.7 = (f32[2,3,64]{2,1,0:T(4,128)S(1)}, f32[2,3,64]{2,1,0:T(4,128)S(1)}, u32[]{:S(2)}, u32[]{:S(2)}) collective-permute-start(f32[2,3,64]{2,1,0:T(4,128)S(1)} %get-tuple-element.92), channel_id=1, source_target_pairs={{1,0},{2,1},{3,2},{4,3},{5,4},{6,5},{7,6},{9,8},{10,9},{11,10},{12... | collective-permute-start | bytes 4616 | tf_op jit(solution)/shard_map/ppermute | solution.py:53
  70.4 6.6 %collective-permute-start.8 = (f32[3,22,64]{2,1,0:T(8,128)S(1)}, f32[3,22,64]{2,1,0:T(8,128)S(1)}, u32[]{:S(2)}, u32[]{:S(2)}) collective-permute-start(f32[3,22,64]{2,1,0:T(8,128)S(1)} %get-tuple-element.87), channel_id=1, source_target_pairs={{0,8},{8,16},{16,24},{24,32},{32,40},{40,48},{48,56},{56,64},{64,7... | collective-permute-start | bytes 50696 | tf_op jit(solution)/shard_map/ppermute | solution.py:53
  75.4 4.7 %collective-permute-start.9 = (f32[3,22,64]{2,1,0:T(8,128)S(1)}, f32[3,22,64]{2,1,0:T(8,128)S(1)}, u32[]{:S(2)}, u32[]{:S(2)}) collective-permute-start(f32[3,22,64]{2,1,0:T(8,128)S(1)} %get-tuple-element.88), channel_id=1, source_target_pairs={{8,0},{16,8},{24,16},{32,24},{40,32},{48,40},{56,48},{64,56},{72,6... | collective-permute-start | bytes 50696 | tf_op jit(solution)/shard_map/ppermute | solution.py:53
where the time goes:
time: 129 us; the launch traced here: 128 us
  blocking collectives  37.1 us (29%)
  starting transfers between devices  31.4 us (24%)
  waiting for transfers between devices  28.8 us (22%)
  other arithmetic  18.3 us (14%)
  local copies, waits for them, and re-layouts  6.72 us (5%)
  matrix products  3.27 us (3%)
  between operations  2.68 us (2%)
    all_gather x1, blocking collectives, collect_grid(): both = lax.all_gather(flat, ('xb', 'yb'), axis=0, tiled=True)  37.1 us
    ppermute x10, starting transfers between devices, exchange(): got = lax.ppermute(joined, axis, pairs)  31.4 us
    ppermute x10, waiting for transfers between devices, exchange(): got = lax.ppermute(joined, axis, pairs)  28.8 us
    add x7, other arithmetic, coarse_solve(): field + jacobi_weight * (right_side - apply_operator(extend(field), field...  4.78 us
    unnamed x21, local copies, waits for them, and re-layouts  4.42 us
    add x3, other arithmetic, smooth_box(): second = trim(first) + second_step  2.77 us
  transfers between devices with their start and end apart: 10, of which 8 were waited for; matrix products, arithmetic and copies ran while one was open for 2% of the time, Pallas kernels for 0%

commit v1 on v0

--- a/solution.py
+++ b/solution.py
@@ -196,7 +196,10 @@
     count_x = lax.axis_size("xb")
     count_y = lax.axis_size("yb")
     flat = jnp.concatenate([right_side.reshape(1, -1), coefficient.reshape(1, -1)], axis=1)
-    both = lax.all_gather(flat, ("xb", "yb"), axis=0, tiled=True)
+    part_next = jax.lax.axis_size(("xb", "yb"))
+    piece_now = jnp.stack(part_next * [flat])
+    local_out = jax.lax.all_to_all(piece_now, ("xb", "yb"), 0, 0)
+    both = jnp.concatenate(local_out, axis=0)
     size = sx * sy * sz
     return tuple(
         (

time: 129 us -> 114 us (0.88)
  blocking collectives: 37.1 us -> 0 us
  starting transfers between devices: 31.4 us -> 42.4 us
  waiting for transfers between devices: 28.8 us -> 38.8 us
    all_gather x1 -> x0, blocking collectives: 37.1 us -> none  [collect_grid(): both = lax.all_gather(flat, ('xb', 'yb'), axis=0, tiled=True)]
    all_to_all x0 -> x1, starting transfers between devices: none -> 11 us  [collect_grid(): local_out = jax.lax.all_to_all(piece_now, ('xb', 'yb'), 0, 0)]
    all_to_all x0 -> x1, waiting for transfers between devices: none -> 9.98 us  [collect_grid(): local_out = jax.lax.all_to_all(piece_now, ('xb', 'yb'), 0, 0)]
  transfers between devices with their start and end apart: 10 -> 11, of which waited for: 8 -> 9; matrix products, arithmetic and copies ran while one was open for 2% -> 2% of each run, Pallas kernels for 0% -> 0%
where the time goes in v1:
time: 114 us; the launch traced here: 113 us
  starting transfers between devices  42.4 us (37%)
  waiting for transfers between devices  38.8 us (34%)
  other arithmetic  18.3 us (16%)
  local copies, waits for them, and re-layouts  7.58 us (7%)
  matrix products  3.28 us (3%)
  between operations  2.71 us (2%)
    ppermute x10, starting transfers between devices, exchange(): got = lax.ppermute(joined, axis, pairs)  31.4 us
    ppermute x10, waiting for transfers between devices, exchange(): got = lax.ppermute(joined, axis, pairs)  28.8 us
    all_to_all x1, starting transfers between devices, collect_grid(): local_out = jax.lax.all_to_all(piece_now, ('xb', 'yb'), 0, 0)  11 us
    all_to_all x1, waiting for transfers between devices, collect_grid(): local_out = jax.lax.all_to_all(piece_now, ('xb', 'yb'), 0, 0)  9.98 us
    add x7, other arithmetic, coarse_solve(): field + jacobi_weight * (right_side - apply_operator(extend(field), field...  4.78 us
    unnamed x21, local copies, waits for them, and re-layouts  4.42 us
    add x3, other arithmetic, smooth_box(): second = trim(first) + second_step  2.77 us
  transfers between devices with their start and end apart: 11, of which 9 were waited for; matrix products, arithmetic and copies ran while one was open for 2% of the time, Pallas kernels for 0%

profile of v1, /device:TPU:1, one launch (start us, length us, event | category | flops | bytes accessed | tf_op | source)
XLA Modules:
  0.0 113.0 jit_solution(6935233193139851123)
XLA Ops:
  0.7 1.0 slice_dynamic-update-slice_fusion.2
  1.7 1.3 %fusion.218 = f32[4,64,128]{2,1,0:T(8,128)S(1)} fusion(f32[4,2,64,256]{3,2,1,0:T(8,128)} %bitcast.80, s32[256]{0:T(256)S(1)} %and_select_fusion.4), kind=kOutput, calls=%fused_computation.335 | convolution fusion | flops 100761600 | bytes 656384 | tf_op jit(solution)/shard_map/xyZ,zZ->xyz/dot_general | solution.py:134
  3.6 0.9 slice_dynamic-update-slice_fusion.1
  4.5 4.5 %collective-permute-start = (f32[30,7,256]{2,1,0:T(8,128)S(1)}, f32[30,7,256]{2,1,0:T(8,128)S(1)}, u32[]{:S(2)}, u32[]{:S(2)}) collective-permute-start(f32[30,7,256]{2,1,0:T(8,128)S(1)} %constant_dynamic-update-slice_fusion), channel_id=1, source_target_pairs={{0,1},{1,2},{2,3},{3,4},{4,5},{5,6},{6,7},{8,9},{9,10},{10,11},{11... | collective-permute-start | bytes 645128 | tf_op jit(solution)/shard_map/ppermute | solution.py:53
  9.1 1.9 %collective-permute-start.1 = (f32[30,7,256]{2,1,0:T(8,128)S(1)}, f32[30,7,256]{2,1,0:T(8,128)S(1)}, u32[]{:S(2)}, u32[]{:S(2)}) collective-permute-start(f32[30,7,256]{2,1,0:T(8,128)S(1)} %constant_dynamic-update-slice_fusion.2), channel_id=1, source_target_pairs={{1,0},{2,1},{3,2},{4,3},{5,4},{6,5},{7,6},{9,8},{10,9},{11,10},{12... | collective-permute-start | bytes 645128 | tf_op jit(solution)/shard_map/ppermute | solution.py:53
  11.0 1.2 %collective-permute-done = f32[30,7,256]{2,1,0:T(8,128)S(1)} collective-permute-done((f32[30,7,256]{2,1,0:T(8,128)S(1)}, f32[30,7,256]{2,1,0:T(8,128)S(1)}, u32[]{:S(2)}, u32[]{:S(2)}) %collective-permute-start) | collective-permute-done | bytes 215072 | tf_op jit(solution)/shard_map/ppermute | solution.py:53
  12.2 0.3 copy_dynamic-update-slice_fusion.1
  12.6 4.0 %collective-permute-done.1 = f32[30,7,256]{2,1,0:T(8,128)S(1)} collective-permute-done((f32[30,7,256]{2,1,0:T(8,128)S(1)}, f32[30,7,256]{2,1,0:T(8,128)S(1)}, u32[]{:S(2)}, u32[]{:S(2)}) %collective-permute-start.1) | collective-permute-done | bytes 215072 | tf_op jit(solution)/shard_map/ppermute | solution.py:53
  16.8 0.3 copy_dynamic-update-slice_fusion
  17.2 0.6 copy-done.2
  17.8 0.3 copy_dynamic-update-slice_fusion.2
  18.5 3.6 %collective-permute-start.2 = (f32[8,78,256]{2,0,1:T(8,128)S(1)}, f32[8,78,256]{2,0,1:T(8,128)S(1)}, u32[]{:S(2)}, u32[]{:S(2)}) collective-permute-start(f32[8,78,256]{2,0,1:T(8,128)S(1)} %pad_maximum_fusion.3), channel_id=1, source_target_pairs={{0,8},{8,16},{16,24},{24,32},{32,40},{40,48},{48,56},{56,64},{64,7... | collective-permute-start | bytes 1916936 | tf_op jit(solution)/shard_map/ppermute | solution.py:53
  22.3 1.3 %collective-permute-start.3 = (f32[8,78,256]{2,0,1:T(8,128)S(1)}, f32[8,78,256]{2,0,1:T(8,128)S(1)}, u32[]{:S(2)}, u32[]{:S(2)}) collective-permute-start(f32[8,78,256]{2,0,1:T(8,128)S(1)} %pad_maximum_fusion.4), channel_id=1, source_target_pairs={{8,0},{16,8},{24,16},{32,24},{40,32},{48,40},{56,48},{64,56},{72,6... | collective-permute-start | bytes 1916936 | tf_op jit(solution)/shard_map/ppermute | solution.py:53
  23.7 8.9 %collective-permute-done.2 = f32[8,78,256]{2,0,1:T(8,128)S(1)} collective-permute-done((f32[8,78,256]{2,0,1:T(8,128)S(1)}, f32[8,78,256]{2,0,1:T(8,128)S(1)}, u32[]{:S(2)}, u32[]{:S(2)}) %collective-permute-start.2) | collective-permute-done | bytes 639008 | tf_op jit(solution)/shard_map/ppermute | solution.py:53
  32.7 4.3 %collective-permute-done.3 = f32[8,78,256]{2,0,1:T(8,128)S(1)} collective-permute-done((f32[8,78,256]{2,0,1:T(8,128)S(1)}, f32[8,78,256]{2,0,1:T(8,128)S(1)}, u32[]{:S(2)}, u32[]{:S(2)}) %collective-permute-start.3) | collective-permute-done | bytes 639008 | tf_op jit(solution)/shard_map/ppermute | solution.py:53
  37.3 1.6 %add_add_fusion = (f32[12,76,256]{2,0,1:T(8,128)S(1)}, f32[12,76,256]{2,0,1:T(8,128)S(1)}, f32[12,76,256]{2,0,1:T(8,128)S(1)}, f32[12,76,256]{2,0,1:T(8,128)S(1)...) fusion(f32[14,78,256]{2,0,1:T(8,128)S(1)} %pad_maximum_fusion.2), kind=kLoop, calls=%fused_computation.55 | loop fusion | flops 5836800 | bytes 14041088 | tf_op jit(solution)/shard_map/add | solution.py:168
  39.5 2.1 %slice_add_fusion.4 = (f32[12,76,256]{2,0,1:T(8,128)S(1)}, f32[12,76,256]{2,0,1:T(8,128)S(1)}) fusion(f32[14,78,256]{2,0,1:T(8,128)S(1)} %pad_maximum_fusion, f32[12,76,256]{2,0,1:T(8,128)S(1)} %get-tuple-element.42, f32[12,76,256]{2,0,1:T(8,128)S(1)} %get-tuple-element.43, f32[12,76,256]{2,0,1:T(8,128)S(1)} %get-tuple-element.41, ...), kind=kLoop, calls=%fused_computation.74 | loop fusion | flops 5369856 | bytes 18087936 | tf_op jit(solution)/shard_map/add | solution.py:181
  41.6 2.4 %fusion.31 = f32[10,74,256]{2,0,1:T(8,128)S(1)} fusion(f32[12,76,256]{2,0,1:T(8,128)S(1)} %get-tuple-element.44, f32[12,76,256]{2,0,1:T(8,128)S(1)} %get-tuple-element.42, f32[12,76,256]{2,0,1:T(8,128)S(1)} %get-tuple-element.43, f32[12,76,256]{2,0,1:T(8,128)S(1)} %get-tuple-element.41, f32[12,76,256]{2,0,1:T(8,128)S(1)} %get-tuple-element.40, ...), kind=kLoop, calls=%fused_computation.63 | loop fusion | flops 3599360 | bytes 18976768 | tf_op jit(solution)/shard_map/add | solution.py:187
  44.0 0.9 fusion.40
  45.0 0.3 reshape.339
  45.3 0.5 fusion.365
  45.8 0.3 fusion.213
  46.5 3.5 %collective-permute-start.4 = (f32[7,38,128]{2,1,0:T(8,128)S(1)}, f32[7,38,128]{2,1,0:T(8,128)S(1)}, u32[]{:S(2)}, u32[]{:S(2)}) collective-permute-start(f32[7,38,128]{2,1,0:T(8,128)S(1)} %get-tuple-element.89), channel_id=1, source_target_pairs={{0,8},{8,16},{16,24},{24,32},{32,40},{40,48},{48,56},{56,64},{64,7... | collective-permute-start | bytes 408584 | tf_op jit(solution)/shard_map/ppermute | solution.py:53
  50.0 1.3 %collective-permute-start.5 = (f32[7,38,128]{2,1,0:T(8,128)S(1)}, f32[7,38,128]{2,1,0:T(8,128)S(1)}, u32[]{:S(2)}, u32[]{:S(2)}) collective-permute-start(f32[7,38,128]{2,1,0:T(8,128)S(1)} %get-tuple-element.90), channel_id=1, source_target_pairs={{8,0},{16,8},{24,16},{32,24},{40,32},{48,40},{56,48},{64,56},{72,6... | collective-permute-start | bytes 408584 | tf_op jit(solution)/shard_map/ppermute | solution.py:53
  51.4 0.6 collective-permute-done.4
  52.0 3.8 %collective-permute-done.5 = f32[7,38,128]{2,1,0:T(8,128)S(1)} collective-permute-done((f32[7,38,128]{2,1,0:T(8,128)S(1)}, f32[7,38,128]{2,1,0:T(8,128)S(1)}, u32[]{:S(2)}, u32[]{:S(2)}) %collective-permute-start.5) | collective-permute-done | bytes 136224 | tf_op jit(solution)/shard_map/ppermute | solution.py:53
  56.3 0.7 fusion.272
  57.3 8.1 %collective-permute-start.6 = (f32[2,3,64]{2,1,0:T(4,128)S(1)}, f32[2,3,64]{2,1,0:T(4,128)S(1)}, u32[]{:S(2)}, u32[]{:S(2)}) collective-permute-start(f32[2,3,64]{2,1,0:T(4,128)S(1)} %get-tuple-element.91), channel_id=1, source_target_pairs={{0,1},{1,2},{2,3},{3,4},{4,5},{5,6},{6,7},{8,9},{9,10},{10,11},{11... | collective-permute-start | bytes 4616 | tf_op jit(solution)/shard_map/ppermute | solution.py:53
  65.4 1.9 %collective-permute-start.7 = (f32[2,3,64]{2,1,0:T(4,128)S(1)}, f32[2,3,64]{2,1,0:T(4,128)S(1)}, u32[]{:S(2)}, u32[]{:S(2)}) collective-permute-start(f32[2,3,64]{2,1,0:T(4,128)S(1)} %get-tuple-element.92), channel_id=1, source_target_pairs={{1,0},{2,1},{3,2},{4,3},{5,4},{6,5},{7,6},{9,8},{10,9},{11,10},{12... | collective-permute-start | bytes 4616 | tf_op jit(solution)/shard_map/ppermute | solution.py:53
  67.4 3.0 %collective-permute-done.7 = f32[2,3,64]{2,1,0:T(4,128)S(1)} collective-permute-done((f32[2,3,64]{2,1,0:T(4,128)S(1)}, f32[2,3,64]{2,1,0:T(4,128)S(1)}, u32[]{:S(2)}, u32[]{:S(2)}) %collective-permute-start.7) | collective-permute-done | bytes 1568 | tf_op jit(solution)/shard_map/ppermute | solution.py:53
  70.4 3.8 %collective-permute-start.8 = (f32[3,22,64]{2,1,0:T(8,128)S(1)}, f32[3,22,64]{2,1,0:T(8,128)S(1)}, u32[]{:S(2)}, u32[]{:S(2)}) collective-permute-start(f32[3,22,64]{2,1,0:T(8,128)S(1)} %get-tuple-element.87), channel_id=1, source_target_pairs={{0,8},{8,16},{16,24},{24,32},{32,40},{40,48},{48,56},{56,64},{64,7... | collective-permute-start | bytes 50696 | tf_op jit(solution)/shard_map/ppermute | solution.py:53
  74.4 1.5 %collective-permute-start.9 = (f32[3,22,64]{2,1,0:T(8,128)S(1)}, f32[3,22,64]{2,1,0:T(8,128)S(1)}, u32[]{:S(2)}, u32[]{:S(2)}) collective-permute-start(f32[3,22,64]{2,1,0:T(8,128)S(1)} %get-tuple-element.88), channel_id=1, source_target_pairs={{8,0},{16,8},{24,16},{32,24},{40,32},{48,40},{56,48},{64,56},{72,6... | collective-permute-start | bytes 50696 | tf_op jit(solution)/shard_map/ppermute | solution.py:53
  76.0 3.1 %collective-permute-done.9 = f32[3,22,64]{2,1,0:T(8,128)S(1)} collective-permute-done((f32[3,22,64]{2,1,0:T(8,128)S(1)}, f32[3,22,64]{2,1,0:T(8,128)S(1)}, u32[]{:S(2)}, u32[]{:S(2)}) %collective-permute-start.9) | collective-permute-done | bytes 16928 | tf_op jit(solution)/shard_map/ppermute | solution.py:53
  79.4 0.6 fusion.311
  80.4 0.9 stack.2
  81.2 11.0 %all-to-all-start = ((f32[128,1,512]{2,1,0:T(1,128)}), f32[128,1,512]{2,1,0:T(1,128)S(1)}, u32[]{:S(2)}, u32[]{:S(2)}) async-start(f32[128,1,512]{2,1,0:T(1,128)} %stack.2), calls=%async_computation | async-start | bytes 524288 | tf_op jit(solution)/shard_map/all_to_all | solution.py:201
  92.3 1.0 copy.24
  93.2 10.0 %all-to-all-done = f32[128,1,512]{2,1,0:T(1,128)S(1)} async-done(((f32[128,1,512]{2,1,0:T(1,128)}), f32[128,1,512]{2,1,0:T(1,128)S(1)}, u32[]{:S(2)}, u32[]{:S(2)}) %all-to-all-start) | async-done | bytes 262176 | tf_op jit(solution)/shard_map/all_to_all | solution.py:201
  103.7 1.0 fusion.192
  104.7 0.7 fusion.68
  105.3 0.7 fusion.84
  106.0 0.7 fusion.100
  106.7 0.7 fusion.116
  107.4 0.7 fusion.132
  108.1 0.7 fusion.148
  108.8 0.7 fusion.164
  109.5 1.6 %fusion.210 = (f32[]{:T(128)}, f32[]{:T(128)}) fusion(f32[16,64,32]{2,1,0:T(8,128)S(1)} %get-tuple-element.11, f32[16,64,32]{2,1,0:T(8,128)S(1)} %broadcast_in_dim.37, f32[16,64,32]{2,1,0:T(8,128)S(1)} %get-tuple-element.12, f32[16,64,32]{2,1,0:T(8,128)S(1)} %get-tuple-element.13, f32[16,64,32]{2,1,0:T(8,128)S(1)} %get-tuple-element.14, ...), kind=kLoop, calls=%fused_computation.320 | loop fusion | flops 1114110 | bytes 1179656 | tf_op jit(solution)/shard_map/reduce_sum | solution.py:153
  112.4 0.6 dynamic-slice_add_fusion
  (93 shorter events, 5.3 us)
Async XLA Ops:
  0.6 3.9 %copy-start = (f32[8,64,256]{2,1,0:T(8,128)S(1)}, f32[8,64,256]{2,1,0:T(8,128)}, u32[]{:S(2)}) copy-start(f32[8,64,256]{2,1,0:T(8,128)} %param.5) | copy-start | bytes 1572868
  0.6 11.6 %copy-start.1 = (f32[8,64,256]{2,1,0:T(8,128)S(1)}, f32[8,64,256]{2,1,0:T(8,128)}, u32[]{:S(2)}) copy-start(f32[8,64,256]{2,1,0:T(8,128)} %param.4) | copy-start | bytes 1572868
  4.5 7.6 %collective-permute-start = (f32[30,7,256]{2,1,0:T(8,128)S(1)}, f32[30,7,256]{2,1,0:T(8,128)S(1)}, u32[]{:S(2)}, u32[]{:S(2)}) collective-permute-start(f32[30,7,256]{2,1,0:T(8,128)S(1)} %constant_dynamic-update-slice_fusion), channel_id=1, source_target_pairs={{0,1},{1,2},{2,3},{3,4},{4,5},{5,6},{6,7},{8,9},{9,10},{10,11},{11... | collective-permute-start | bytes 645128 | tf_op jit(solution)/shard_map/ppermute | solution.py:53
  9.1 7.5 %collective-permute-start.1 = (f32[30,7,256]{2,1,0:T(8,128)S(1)}, f32[30,7,256]{2,1,0:T(8,128)S(1)}, u32[]{:S(2)}, u32[]{:S(2)}) collective-permute-start(f32[30,7,256]{2,1,0:T(8,128)S(1)} %constant_dynamic-update-slice_fusion.2), channel_id=1, source_target_pairs={{1,0},{2,1},{3,2},{4,3},{5,4},{6,5},{7,6},{9,8},{10,9},{11,10},{12... | collective-permute-start | bytes 645128 | tf_op jit(solution)/shard_map/ppermute | solution.py:53
  16.7 1.0 copy-start.2
  18.5 14.1 %collective-permute-start.2 = (f32[8,78,256]{2,0,1:T(8,128)S(1)}, f32[8,78,256]{2,0,1:T(8,128)S(1)}, u32[]{:S(2)}, u32[]{:S(2)}) collective-permute-start(f32[8,78,256]{2,0,1:T(8,128)S(1)} %pad_maximum_fusion.3), channel_id=1, source_target_pairs={{0,8},{8,16},{16,24},{24,32},{32,40},{40,48},{48,56},{56,64},{64,7... | collective-permute-start | bytes 1916936 | tf_op jit(solution)/shard_map/ppermute | solution.py:53
  22.3 14.6 %collective-permute-start.3 = (f32[8,78,256]{2,0,1:T(8,128)S(1)}, f32[8,78,256]{2,0,1:T(8,128)S(1)}, u32[]{:S(2)}, u32[]{:S(2)}) collective-permute-start(f32[8,78,256]{2,0,1:T(8,128)S(1)} %pad_maximum_fusion.4), channel_id=1, source_target_pairs={{8,0},{16,8},{24,16},{32,24},{40,32},{48,40},{56,48},{64,56},{72,6... | collective-permute-start | bytes 1916936 | tf_op jit(solution)/shard_map/ppermute | solution.py:53
  46.5 5.6 %collective-permute-start.4 = (f32[7,38,128]{2,1,0:T(8,128)S(1)}, f32[7,38,128]{2,1,0:T(8,128)S(1)}, u32[]{:S(2)}, u32[]{:S(2)}) collective-permute-start(f32[7,38,128]{2,1,0:T(8,128)S(1)} %get-tuple-element.89), channel_id=1, source_target_pairs={{0,8},{8,16},{16,24},{24,32},{32,40},{40,48},{48,56},{56,64},{64,7... | collective-permute-start | bytes 408584 | tf_op jit(solution)/shard_map/ppermute | solution.py:53
  50.0 5.8 %collective-permute-start.5 = (f32[7,38,128]{2,1,0:T(8,128)S(1)}, f32[7,38,128]{2,1,0:T(8,128)S(1)}, u32[]{:S(2)}, u32[]{:S(2)}) collective-permute-start(f32[7,38,128]{2,1,0:T(8,128)S(1)} %get-tuple-element.90), channel_id=1, source_target_pairs={{8,0},{16,8},{24,16},{32,24},{40,32},{48,40},{56,48},{64,56},{72,6... | collective-permute-start | bytes 408584 | tf_op jit(solution)/shard_map/ppermute | solution.py:53
  57.3 10.0 %collective-permute-start.6 = (f32[2,3,64]{2,1,0:T(4,128)S(1)}, f32[2,3,64]{2,1,0:T(4,128)S(1)}, u32[]{:S(2)}, u32[]{:S(2)}) collective-permute-start(f32[2,3,64]{2,1,0:T(4,128)S(1)} %get-tuple-element.91), channel_id=1, source_target_pairs={{0,1},{1,2},{2,3},{3,4},{4,5},{5,6},{6,7},{8,9},{9,10},{10,11},{11... | collective-permute-start | bytes 4616 | tf_op jit(solution)/shard_map/ppermute | solution.py:53
  65.4 4.9 %collective-permute-start.7 = (f32[2,3,64]{2,1,0:T(4,128)S(1)}, f32[2,3,64]{2,1,0:T(4,128)S(1)}, u32[]{:S(2)}, u32[]{:S(2)}) collective-permute-start(f32[2,3,64]{2,1,0:T(4,128)S(1)} %get-tuple-element.92), channel_id=1, source_target_pairs={{1,0},{2,1},{3,2},{4,3},{5,4},{6,5},{7,6},{9,8},{10,9},{11,10},{12... | collective-permute-start | bytes 4616 | tf_op jit(solution)/shard_map/ppermute | solution.py:53
  70.4 5.5 %collective-permute-start.8 = (f32[3,22,64]{2,1,0:T(8,128)S(1)}, f32[3,22,64]{2,1,0:T(8,128)S(1)}, u32[]{:S(2)}, u32[]{:S(2)}) collective-permute-start(f32[3,22,64]{2,1,0:T(8,128)S(1)} %get-tuple-element.87), channel_id=1, source_target_pairs={{0,8},{8,16},{16,24},{24,32},{32,40},{40,48},{48,56},{56,64},{64,7... | collective-permute-start | bytes 50696 | tf_op jit(solution)/shard_map/ppermute | solution.py:53
  74.4 4.7 %collective-permute-start.9 = (f32[3,22,64]{2,1,0:T(8,128)S(1)}, f32[3,22,64]{2,1,0:T(8,128)S(1)}, u32[]{:S(2)}, u32[]{:S(2)}) collective-permute-start(f32[3,22,64]{2,1,0:T(8,128)S(1)} %get-tuple-element.88), channel_id=1, source_target_pairs={{8,0},{16,8},{24,16},{32,24},{40,32},{48,40},{56,48},{64,56},{72,6... | collective-permute-start | bytes 50696 | tf_op jit(solution)/shard_map/ppermute | solution.py:53
  81.2 22.0 %all-to-all-start = ((f32[128,1,512]{2,1,0:T(1,128)}), f32[128,1,512]{2,1,0:T(1,128)S(1)}, u32[]{:S(2)}, u32[]{:S(2)}) async-start(f32[128,1,512]{2,1,0:T(1,128)} %stack.2), calls=%async_computation | async-start | bytes 524288 | tf_op jit(solution)/shard_map/all_to_all | solution.py:201
